TPU v7x, 512 devices: a whole 4x8x8 slice. The times are simulated.
512 devices in a mesh: dp: 32 (over z, y_lo, core), feat: 16 (over y_hi, x).
Axes of the slice: x: 4, y: 8 (y_hi: 4, y_lo: 2; y = y_hi * 2 + y_lo), z: 8, core: 2. Of those that a mesh axis runs over, the one named last changes fastest.
Arguments:
- tokens: bfloat16 [8192, 8192], P('dp', 'feat'), may hold values from -6 to 6
- up_left: bfloat16 [16, 512, 2048], P('feat', 'dp'), may hold values from -0.25 to 0.25
- up_right: bfloat16 [2048, 16, 16], P('feat'), may hold values from -1.5 to 1.5
- down_left: bfloat16 [16, 2048, 512], P('feat', 'dp'), may hold values from -0.125 to 0.125
- down_right: bfloat16 [512, 16, 16], P('feat'), may hold values from -1.5 to 1.5
- layer_grad: bfloat16 [8192, 8192], P('dp', 'feat'), may hold values from -6 to 6
Outputs:
- layer_out: bfloat16 [8192, 8192], P('dp', 'feat')
- grad_tokens: bfloat16 [8192, 8192], P('dp', 'feat')
- grad_up_left: float32 [16, 512, 2048], P('feat', 'dp')
- grad_up_right: float32 [2048, 16, 16], P('feat')
- grad_down_left: float32 [16, 2048, 512], P('feat', 'dp')
- grad_down_right: float32 [512, 16, 16], P('feat')
All inputs are finite; a program needn't handle non-finite values.
Results may differ from a plain program's by a relative error of at most 0.0067.
Values may be sent and summed in bfloat16 or wider, within the bound.
No kernel may reach another device: no remote copies, remote signals or barrier semaphores. Data moves between devices by JAX's collectives and lax.ppermute only.
A program may use at most 128 MiB of HBM per device.

v0:
```python
import jax
import jax.numpy as jnp
import numpy as np
from jax import lax
from jax.sharding import Mesh
from jax.sharding import PartitionSpec as P

TILE_UP = 128
TILE_DOWN = 32
DP_AXES = ("z", "ylo", "core")
FEAT_AXES = ("yhi", "x")


def split_mesh(mesh):
    n_dp = mesh.shape["dp"]
    n_feat = mesh.shape["feat"]
    sizes = (n_dp // 4, 2, 2, n_feat // 4, 4)
    devices = np.asarray(mesh.devices).reshape(sizes)
    return Mesh(devices, DP_AXES + FEAT_AXES)


def exchange(wired):
    rows, feat_count, piece = wired.shape
    n_x = lax.axis_size("x")
    n_y = feat_count // n_x
    shaped = wired.reshape(rows, n_y, n_x, piece)
    shaped = lax.all_to_all(shaped, "x", 2, 2, tiled=True)
    shaped = lax.all_to_all(shaped, "yhi", 1, 1, tiled=True)
    return shaped.reshape(rows, feat_count, piece)


def dp_reduce_scatter(part, row_axis):
    shape = part.shape
    rows = shape[row_axis]
    n_z = lax.axis_size("z")
    split = shape[:row_axis] + (n_z, 2, 2, rows // (4 * n_z)) + shape[row_axis + 1 :]
    x = part.reshape(split)
    x = lax.psum_scatter(x, "core", scatter_dimension=row_axis + 2, tiled=True)
    x = lax.psum_scatter(x, "z", scatter_dimension=row_axis, tiled=True)
    x = lax.psum_scatter(x, "ylo", scatter_dimension=row_axis + 1, tiled=True)
    return x.reshape(shape[:row_axis] + (rows // (4 * n_z),) + shape[row_axis + 1 :])


def dp_all_gather(local, row_axis):
    shape = local.shape
    rows = shape[row_axis]
    x = local.reshape(shape[:row_axis] + (1, 1, 1, rows) + shape[row_axis + 1 :])
    x = lax.all_gather(x, "ylo", axis=row_axis + 1, tiled=True)
    x = lax.all_gather(x, "z", axis=row_axis, tiled=True)
    x = lax.all_gather(x, "core", axis=row_axis + 2, tiled=True)
    total = x.shape[row_axis] * x.shape[row_axis + 1] * x.shape[row_axis + 2] * rows
    return x.reshape(shape[:row_axis] + (total,) + shape[row_axis + 1 :])


def to_wire(blocks, feat_count):
    tok_rows, local_blocks, full_width = blocks.shape
    piece = full_width // feat_count
    shaped = blocks.reshape(tok_rows, local_blocks, feat_count, piece).transpose(0, 2, 1, 3)
    return shaped.reshape(tok_rows, feat_count, local_blocks * piece)


def from_wire(wired, local_blocks):
    tok_rows, feat_count, line_len = wired.shape
    piece = line_len // local_blocks
    shaped = wired.reshape(tok_rows, feat_count, local_blocks, piece).transpose(0, 2, 1, 3)
    return shaped.reshape(tok_rows, local_blocks, feat_count * piece)


def on_device(tokens, up_left, up_right, down_left, down_right, layer_grad):
    tok_rows = tokens.shape[0]
    local_blocks = up_left.shape[0]
    hidden_width = up_left.shape[2]
    block_width = down_left.shape[2]
    blocks_all = up_right.shape[1]
    group_up = up_right.shape[0]
    group_down = down_right.shape[0]
    feat_count = lax.axis_size("yhi") * lax.axis_size("x")
    n_dp = lax.axis_size("z") * lax.axis_size("ylo") * lax.axis_size("core")
    grad_scale = float(tok_rows * n_dp) ** (-0.5)
    tiles_up = group_up // TILE_UP
    tiles_down = group_down // TILE_DOWN
    up_full = dp_all_gather(up_left, 1)
    token_blocks = tokens.reshape(tok_rows, local_blocks, block_width)
    up_inner = jnp.einsum(
        "tbi,big->tbg", token_blocks, up_full, preferred_element_type=jnp.float32
    ).astype(jnp.bfloat16)
    up_mixed = exchange(to_wire(up_inner, feat_count))
    preact = jnp.einsum("tjg,gjk->tkg", up_mixed, up_right, preferred_element_type=jnp.float32)
    sigmoid_val = jax.nn.sigmoid(preact)
    activated = (
        (preact * sigmoid_val)
        .reshape(tok_rows, blocks_all, tiles_up, TILE_UP)
        .transpose(0, 2, 1, 3)
    )
    hidden = activated.reshape(tok_rows, local_blocks, hidden_width).astype(jnp.bfloat16)
    down_full = dp_all_gather(down_left, 1)
    down_inner = jnp.einsum(
        "tbh,bhc->tbc", hidden, down_full, preferred_element_type=jnp.float32
    ).astype(jnp.bfloat16)
    down_mixed = exchange(to_wire(down_inner, feat_count)).reshape(
        tok_rows, blocks_all * group_down
    )
    identity = jnp.eye(group_down, dtype=jnp.bfloat16).reshape(group_down, tiles_down, TILE_DOWN)
    mix_matrix = jnp.einsum(
        "cjk,cal->jcakl", down_right, identity, preferred_element_type=jnp.float32
    )
    mix_matrix = mix_matrix.astype(jnp.bfloat16).reshape(
        blocks_all * group_down, blocks_all * group_down
    )
    layer_out = jnp.dot(down_mixed, mix_matrix, preferred_element_type=jnp.float32).astype(
        jnp.bfloat16
    )
    grad_down_mixed = lax.dot_general(
        layer_grad, mix_matrix, (((1,), (1,)), ((), ())), preferred_element_type=jnp.float32
    ).astype(jnp.bfloat16)
    grad_by_group = layer_grad.reshape(tok_rows, tiles_down, blocks_all, TILE_DOWN).transpose(
        0, 2, 1, 3
    )
    grad_by_group = grad_by_group.reshape(tok_rows, blocks_all, group_down)
    right_down_term = (
        jnp.einsum(
            "tjc,tkc->cjk",
            down_mixed.reshape(tok_rows, blocks_all, group_down),
            grad_by_group,
            preferred_element_type=jnp.float32,
        )
        * grad_scale
    )
    grad_down_inner = from_wire(
        exchange(grad_down_mixed.reshape(tok_rows, feat_count, local_blocks * group_down)),
        local_blocks,
    )
    grad_down_left = dp_reduce_scatter(
        jnp.einsum("tbh,tbc->hbc", hidden, grad_down_inner, preferred_element_type=jnp.float32)
        * grad_scale,
        0,
    ).transpose(1, 0, 2)
    grad_hidden = jnp.einsum(
        "tbc,bhc->tbh", grad_down_inner, down_full, preferred_element_type=jnp.float32
    )
    grad_hidden = grad_hidden.reshape(tok_rows, tiles_up, blocks_all, TILE_UP).transpose(0, 2, 1, 3)
    grad_hidden = grad_hidden.reshape(tok_rows, blocks_all, group_up)
    grad_preact = (grad_hidden * sigmoid_val * (1.0 + preact * (1.0 - sigmoid_val))).astype(
        jnp.bfloat16
    )
    grad_up_mixed = jnp.einsum(
        "tkg,gjk->tjg", grad_preact, up_right, preferred_element_type=jnp.float32
    ).astype(jnp.bfloat16)
    right_up_term = (
        jnp.einsum("tjg,tkg->gjk", up_mixed, grad_preact, preferred_element_type=jnp.float32)
        * grad_scale
    )
    grad_up_inner = from_wire(exchange(grad_up_mixed), local_blocks)
    grad_tokens = jnp.einsum(
        "tbg,big->tbi", grad_up_inner, up_full, preferred_element_type=jnp.float32
    ).astype(jnp.bfloat16)
    grad_tokens = grad_tokens.reshape(tok_rows, local_blocks * block_width)
    grad_up_left = dp_reduce_scatter(
        jnp.einsum("tbi,tbg->ibg", token_blocks, grad_up_inner, preferred_element_type=jnp.float32)
        * grad_scale,
        0,
    ).transpose(1, 0, 2)
    rights = jnp.concatenate([right_up_term, right_down_term], axis=0)
    rights = lax.psum(rights, DP_AXES)
    grad_up_right = rights[:group_up]
    grad_down_right = rights[group_up:]
    return (layer_out, grad_tokens, grad_up_left, grad_up_right, grad_down_left, grad_down_right)


def solution(mesh):
    fine = split_mesh(mesh)
    row = P(DP_AXES, FEAT_AXES)
    weight = P(FEAT_AXES, DP_AXES, None)
    mixer = P(FEAT_AXES, None, None)
    return jax.shard_map(
        on_device,
        mesh=fine,
        in_specs=(row, weight, mixer, weight, mixer, row),
        out_specs=(row, row, weight, mixer, weight, mixer),
        check_vma=False,
    )
```

profile of v0, /device:TPU:1, one launch (start us, length us, event | category | flops | bytes accessed | tf_op | source)
XLA Modules:
  0.0 650.3 jit_solution(2913419054008153790)
XLA Ops:
  7.2 6.3 all-gather
  13.6 42.4 %all-gather.13.cloned.1.call-done = bf16[16,16,2048]{2,1,0:T(8,128)(2,1)} async-done(((bf16[2,16,2048]{2,1,0:T(8,128)(2,1)}), bf16[16,16,2048]{2,1,0:T(8,128)(2,1)}) %all-gather.13.cloned.1.call-update) | async-done | bytes 1048592 | tf_op jit(solution)/shard_map/all_gather | solution.py:49
  56.1 5.3 all-gather.2
  61.4 0.9 copy.89
  62.4 1.4 fusion
  63.8 2.1 reshape.98
  65.8 0.3 convolution_convert_fusion.3
  66.2 0.7 copy.90
  66.9 4.0 all-to-all-start.4
  70.8 10.1 %all-gather.9.cloned.1.call-done = bf16[1,8,2,2,16,2048]{5,4,3,2,1,0:T(8,128)(2,1)} async-done(((bf16[1,8,2,1,16,2048]{5,4,3,2,1,0:T(8,128)(2,1)}), bf16[1,8,2,2,16,2048]{5,4,3,2,1,0:T(8,128)(2,1)}) %all-gather.9.cloned.1.call-update) | async-done | bytes 2097168 | tf_op jit(solution)/shard_map/all_gather | solution.py:50
  80.9 2.3 convolution_convert_fusion
  83.3 1.1 copy.81
  84.4 3.5 all-to-all-start
  87.9 32.6 %all-gather.15.cloned.1.call-done = bf16[16,64,512]{2,1,0:T(8,128)(2,1)} async-done(((bf16[2,64,512]{2,1,0:T(8,128)(2,1)}), bf16[16,64,512]{2,1,0:T(8,128)(2,1)}) %all-gather.15.cloned.1.call-update) | async-done | bytes 1048592 | tf_op jit(solution)/shard_map/all_gather | solution.py:49
  120.6 0.7 copy.91
  121.3 6.5 all-to-all-start.5
  127.8 1.0 copy.82
  128.8 6.9 %all-to-all-done.5 = bf16[256,4,4,32]{0,3,2,1:T(8,128)(2,1)S(1)} async-done(((bf16[256,4,4,32]{0,3,2,1:T(8,128)(2,1)}), bf16[256,4,4,32]{0,3,2,1:T(8,128)(2,1)S(1)}, u32[]{:S(2)}, u32[]{:S(2)}) %all-to-all-start.5) | async-done | bytes 262176 | tf_op jit(solution)/shard_map/all_to_all | solution.py:28
  135.7 4.3 all-to-all-start.1
  140.0 1.2 copy.94
  141.2 4.1 all-gather.11.cloned.1.call-done
  145.3 2.3 fusion.16
  147.6 18.1 %all-to-all-done.1 = bf16[256,4,4,128]{0,3,2,1:T(8,128)(2,1)} async-done(((bf16[256,4,4,128]{0,3,2,1:T(8,128)(2,1)}), bf16[256,4,4,128]{0,3,2,1:T(8,128)(2,1)}, u32[]{:S(2)}, u32[]{:S(2)}) %all-to-all-start.1) | async-done | bytes 1048608 | tf_op jit(solution)/shard_map/all_to_all | solution.py:28
  165.8 4.5 fusion.7
  170.2 1.0 copy-done.2
  171.2 0.4 fusion.8
  171.7 0.3 reshape.100
  172.0 0.3 copy.95
  172.3 15.0 %all_to_all.40 = bf16[256,4,4,128]{0,3,1,2:T(8,128)(2,1)S(1)} all-to-all(bf16[256,4,4,128]{0,3,1,2:T(8,128)(2,1)S(1)} %copy.95), channel_id=1, replica_groups=mesh['z'=8,'ylo'=2,'core'=2,'yhi'=4,'x'=4] {'x'}, dimensions={2} | all-to-all | bytes 2097152 | tf_op jit(solution)/shard_map/all_to_all | solution.py:27
  187.3 1.0 copy.96
  188.4 6.5 %all-to-all-start.7 = ((bf16[256,4,4,128]{0,3,2,1:T(8,128)(2,1)}), bf16[256,4,4,128]{0,3,2,1:T(8,128)(2,1)S(1)}, u32[]{:S(2)}, u32[]{:S(2)}) async-start(bf16[256,4,4,128]{0,3,2,1:T(8,128)(2,1)} %copy.96), calls=%async_computation.7 | async-start | bytes 2097152 | tf_op jit(solution)/shard_map/all_to_all | solution.py:28
  194.9 0.3 copy.85
  195.2 1.1 copy-done.6
  196.3 2.7 multiply_bitcast_fusion
  199.0 5.4 copy.103
  204.5 10.2 %all-to-all-done.7 = bf16[256,4,4,128]{0,3,2,1:T(8,128)(2,1)S(1)} async-done(((bf16[256,4,4,128]{0,3,2,1:T(8,128)(2,1)}), bf16[256,4,4,128]{0,3,2,1:T(8,128)(2,1)S(1)}, u32[]{:S(2)}, u32[]{:S(2)}) %all-to-all-start.7) | async-done | bytes 1048608 | tf_op jit(solution)/shard_map/all_to_all | solution.py:28
  214.7 2.7 convolution_multiply_fusion
  217.4 0.0 reduce-scatter.13.cloned.1.call-start
  217.4 1.3 dynamic-slice
  218.7 53.0 %all-reduce.8.cloned.1.call-done = (f32[8,2,2,16,1,2048]{5,3,4,2,1,0:T(8,128)}, f32[8,2,2,64,1,512]{5,3,2,1,0,4:T(8,128)}) async-done(((f32[8,2,2,16,1,2048]{5,3,4,2,1,0:T(8,128)}, f32[8,2,2,64,1,512]{5,3,2,1,0,4:T(8,128)}), (f32[8,2,2,16,1,2048]{5,3,4,2,1,0:T(8,128)}, f32[8,2,2,64,1,512]{5,3,2,1,0,4:T(8,128)})) %all-reduce.8.cloned.1.call-update) | async-done | bytes 8388624
  271.7 3.9 constant_dynamic-slice_fusion
  275.6 3.9 constant_dynamic-slice_fusion.1
  279.5 1.6 copy-done.1
  281.1 1.9 fusion.9
  283.1 0.1 copy.86
  283.2 9.2 %all_to_all.41 = bf16[256,4,4,32]{0,3,1,2:T(8,128)(2,1)S(1)} all-to-all(bf16[256,4,4,32]{0,3,1,2:T(8,128)(2,1)S(1)} %copy.87), channel_id=1, replica_groups=mesh['z'=8,'ylo'=2,'core'=2,'yhi'=4,'x'=4] {'x'}, dimensions={2} | all-to-all | bytes 524288 | tf_op jit(solution)/shard_map/all_to_all | solution.py:27
  292.4 0.7 copy.88
  293.1 6.5 all-to-all-start.3
  299.6 0.8 copy.99
  300.4 2.0 convolution_multiply_fusion.1
  302.5 0.4 copy.101
  302.9 5.1 all-to-all-done.3
  308.0 0.4 convolution_multiply_fusion.2
  308.4 0.2 copy.102
  308.5 0.7 pad_maximum_fusion
  309.3 7.6 %reduce-scatter.13.cloned.1.call-done = f32[1,2,1,64,1,512]{5,3,2,1,0,4:T(8,128)} async-done(((f32[8,2,1,64,1,512]{5,3,2,1,0,4:T(8,128)}), f32[1,2,1,64,1,512]{5,3,2,1,0,4:T(8,128)}) %reduce-scatter.13.cloned.1.call-update) | async-done | bytes 262160 | tf_op jit(solution)/shard_map/reduce_scatter | solution.py:39
  317.0 46.2 %reduce-scatter.9.cloned.1.call-done = f32[1,2,1,16,1,2048]{5,3,4,2,1,0:T(8,128)} async-done(((f32[8,2,1,16,1,2048]{5,3,4,2,1,0:T(8,128)}), f32[1,2,1,16,1,2048]{5,3,4,2,1,0:T(8,128)}) %reduce-scatter.9.cloned.1.call-update) | async-done | bytes 262160 | tf_op jit(solution)/shard_map/reduce_scatter | solution.py:39
  363.3 1.0 convolution_convert_fusion.4
  364.3 233.1 %all-reduce.6.cloned.1.call-done = f32[160,16,16]{0,2,1:T(8,128)} async-done(((f32[160,16,16]{0,2,1:T(8,128)}), f32[160,16,16]{0,2,1:T(8,128)}) %all-reduce.6.cloned.1.call-update) | async-done | bytes 163856 | tf_op jit(solution)/shard_map/psum | solution.py:164
  597.4 1.6 slice.9
  599.0 1.6 slice.8
  600.6 3.0 convolution_convert_fusion.2
  603.6 16.7 %reduce-scatter.15.cloned.1.call-done = f32[1,1,1,64,1,512]{5,3,2,1,0,4:T(8,128)} async-done(((f32[1,2,1,64,1,512]{5,3,2,1,0,4:T(8,128)}), f32[1,1,1,64,1,512]{5,3,2,1,0,4:T(8,128)}) %reduce-scatter.15.cloned.1.call-update) | async-done | bytes 131088 | tf_op jit(solution)/shard_map/reduce_scatter | solution.py:40
  620.3 23.2 %reduce-scatter.11.cloned.1.call-done = f32[1,1,1,16,1,2048]{5,3,4,2,1,0:T(8,128)} async-done(((f32[1,2,1,16,1,2048]{5,3,4,2,1,0:T(8,128)}), f32[1,1,1,16,1,2048]{5,3,4,2,1,0:T(8,128)}) %reduce-scatter.11.cloned.1.call-update) | async-done | bytes 131088 | tf_op jit(solution)/shard_map/reduce_scatter | solution.py:40
  (44 shorter events, 0.5 us)
Async XLA Ops:
  7.2 73.8 %copy-start = (bf16[256,512]{1,0:T(8,128)(2,1)S(1)}, bf16[256,512]{1,0:T(8,128)(2,1)}, u32[]{:S(2)}) copy-start(bf16[256,512]{1,0:T(8,128)(2,1)} %param.6) | copy-start | bytes 786436
  7.2 48.8 %all-gather.13.cloned.1.call-start = ((), (), s32[]{:S(2)}) async-start(), calls=%async_computation.19 | async-start | bytes 1179648 | tf_op jit(solution)/shard_map/all_gather | solution.py:49
  13.6 67.3 %all-gather.9.cloned.1.call-start = ((), (), s32[]{:S(2)}) async-start(), calls=%async_computation.12 | async-start | bytes 3145728 | tf_op jit(solution)/shard_map/all_gather | solution.py:50
  56.0 64.5 %all-gather.15.cloned.1.call-start = ((), (), s32[]{:S(2)}) async-start(), calls=%async_computation.20 | async-start | bytes 1179648 | tf_op jit(solution)/shard_map/all_gather | solution.py:49
  62.3 3.5 copy-start.9
  66.9 17.5 %all-to-all-start.4 = ((bf16[256,4,4,32]{0,3,1,2:T(8,128)(2,1)}), bf16[256,4,4,32]{0,3,1,2:T(8,128)(2,1)S(1)}, u32[]{:S(2)}, u32[]{:S(2)}) async-start(bf16[256,4,4,32]{0,3,1,2:T(8,128)(2,1)} %copy.90), calls=%async_computation.4 | async-start | bytes 524288 | tf_op jit(solution)/shard_map/all_to_all | solution.py:27
  84.4 37.0 %all-to-all-start = ((bf16[256,4,4,128]{0,3,1,2:T(8,128)(2,1)}), bf16[256,4,4,128]{0,3,1,2:T(8,128)(2,1)S(1)}, u32[]{:S(2)}, u32[]{:S(2)}) async-start(bf16[256,4,4,128]{0,3,1,2:T(8,128)(2,1)} %copy.81), calls=%async_computation | async-start | bytes 2097152 | tf_op jit(solution)/shard_map/all_to_all | solution.py:27
  87.9 57.4 %all-gather.11.cloned.1.call-start = ((), (), s32[]{:S(2)}) async-start(), calls=%async_computation.13 | async-start | bytes 3145728 | tf_op jit(solution)/shard_map/all_gather | solution.py:50
  121.3 14.4 %all-to-all-start.5 = ((bf16[256,4,4,32]{0,3,2,1:T(8,128)(2,1)}), bf16[256,4,4,32]{0,3,2,1:T(8,128)(2,1)S(1)}, u32[]{:S(2)}, u32[]{:S(2)}) async-start(bf16[256,4,4,32]{0,3,2,1:T(8,128)(2,1)} %copy.91), calls=%async_computation.5 | async-start | bytes 524288 | tf_op jit(solution)/shard_map/all_to_all | solution.py:28
  127.8 12.2 %copy-start.11 = (bf16[128,16,16]{0,2,1:T(8,128)(2,1)S(1)}, bf16[128,16,16]{0,2,1:T(8,128)(2,1)}, u32[]{:S(2)}) copy-start(bf16[128,16,16]{0,2,1:T(8,128)(2,1)} %param.8) | copy-start | bytes 196612
  135.7 30.0 %all-to-all-start.1 = ((bf16[256,4,4,128]{0,3,2,1:T(8,128)(2,1)}), bf16[256,4,4,128]{0,3,2,1:T(8,128)(2,1)}, u32[]{:S(2)}, u32[]{:S(2)}) async-start(bf16[256,4,4,128]{0,3,2,1:T(8,128)(2,1)} %copy.82), calls=%async_computation.1 | async-start | bytes 2097152 | tf_op jit(solution)/shard_map/all_to_all | solution.py:28
  165.7 5.5 copy-start.7
  170.2 1.0 copy-start.2
  187.3 7.6 %copy-start.8 = (bf16[256,16,128]{0,1,2:T(8,128)(2,1)S(1)}, bf16[256,16,128]{0,1,2:T(8,128)(2,1)}, u32[]{:S(2)}) copy-start(bf16[256,16,128]{0,1,2:T(8,128)(2,1)} %get-tuple-element.21) | copy-start | bytes 3145732
  188.4 26.3 %all-to-all-start.7 = ((bf16[256,4,4,128]{0,3,2,1:T(8,128)(2,1)}), bf16[256,4,4,128]{0,3,2,1:T(8,128)(2,1)S(1)}, u32[]{:S(2)}, u32[]{:S(2)}) async-start(bf16[256,4,4,128]{0,3,2,1:T(8,128)(2,1)} %copy.96), calls=%async_computation.7 | async-start | bytes 2097152 | tf_op jit(solution)/shard_map/all_to_all | solution.py:28
  194.9 76.8 %all-reduce.8.cloned.1.call-start = ((), (), s32[]{:S(2)}) async-start(), calls=%async_computation.21 | async-start | bytes 16777216
  195.2 1.1 copy-start.6
  214.7 2.7 copy-start.4
  217.4 99.6 %reduce-scatter.13.cloned.1.call-start = ((), (), s32[]{:S(2)}) async-start(), calls=%async_computation.17 | async-start | bytes 2359296 | tf_op jit(solution)/shard_map/reduce_scatter | solution.py:39
  275.6 87.7 %reduce-scatter.9.cloned.1.call-start = ((), (), s32[]{:S(2)}) async-start(), calls=%async_computation.14 | async-start | bytes 2359296 | tf_op jit(solution)/shard_map/reduce_scatter | solution.py:39
  279.5 1.6 copy-start.1
  283.1 17.4 %copy-start.3 = (bf16[256,16,128]{0,1,2:T(8,128)(2,1)S(1)}, bf16[256,16,128]{0,1,2:T(8,128)(2,1)}, u32[]{:S(2)}) copy-start(bf16[256,16,128]{0,1,2:T(8,128)(2,1)} %copy-done.2) | copy-start | bytes 3145732
  293.1 14.8 %all-to-all-start.3 = ((bf16[256,4,4,32]{0,3,2,1:T(8,128)(2,1)}), bf16[256,4,4,32]{0,3,2,1:T(8,128)(2,1)S(1)}, u32[]{:S(2)}, u32[]{:S(2)}) async-start(bf16[256,4,4,32]{0,3,2,1:T(8,128)(2,1)} %copy.88), calls=%async_computation.3 | async-start | bytes 524288 | tf_op jit(solution)/shard_map/all_to_all | solution.py:28
  299.6 297.9 %all-reduce.6.cloned.1.call-start = ((), (), s32[]{:S(2)}) async-start(), calls=%async_computation.16 | async-start | bytes 524288 | tf_op jit(solution)/shard_map/psum | solution.py:164
  300.4 7.5 %copy-start.10 = (bf16[256,512]{0,1:T(8,128)(2,1)S(1)}, bf16[256,512]{0,1:T(8,128)(2,1)}, u32[]{:S(2)}) copy-start(bf16[256,512]{0,1:T(8,128)(2,1)} %copy.99) | copy-start | bytes 786436
  302.9 297.7 %copy-start.5 = (bf16[256,4,4,128]{0,3,2,1:T(8,128)(2,1)S(1)}, bf16[256,4,4,128]{0,3,2,1:T(8,128)(2,1)}, u32[]{:S(2)}) copy-start(bf16[256,4,4,128]{0,3,2,1:T(8,128)(2,1)} %copy-done.4) | copy-start | bytes 3145732
  309.3 311.0 %reduce-scatter.15.cloned.1.call-start = ((), (), s32[]{:S(2)}) async-start(), calls=%async_computation.18 | async-start | bytes 393216 | tf_op jit(solution)/shard_map/reduce_scatter | solution.py:40
  317.0 326.5 %reduce-scatter.11.cloned.1.call-start = ((), (), s32[]{:S(2)}) async-start(), calls=%async_computation.15 | async-start | bytes 393216 | tf_op jit(solution)/shard_map/reduce_scatter | solution.py:40
Sparse Core Ops, SparseCore 0:
  13.7 42.2 all-gather.12
  58.1 22.8 all-gather.8
  83.0 37.5 all-gather.14
  122.5 22.7 all-gather.10
  217.5 54.1 all-reduce.7
  275.7 41.1 reduce-scatter.12
  319.8 43.4 reduce-scatter.8
  366.7 230.6 all-reduce.5
  601.0 19.2 reduce-scatter.14
  623.5 19.9 reduce-scatter.10
where the time goes:
time: 652 us; the launch traced here: 650 us
  waiting for transfers between devices  509 us (78%)
  blocking collectives  35.8 us (5%)
  local copies, waits for them, and re-layouts  33.3 us (5%)
  starting transfers between devices  31.5 us (5%)
  matrix products  23.7 us (4%)
  between operations  14.3 us (2%)
    psum x1, waiting for transfers between devices, on_device(): rights = lax.psum(rights, DP_AXES)  233 us
    all_gather x2, waiting for transfers between devices, dp_all_gather(): x = lax.all_gather(x, 'z', axis=row_axis, tiled=True)  75 us
    reduce_scatter x2, waiting for transfers between devices, dp_reduce_scatter(): x = lax.psum_scatter(x, 'z', scatter_dimension=row_axis, tiled=True)  53.9 us
    unnamed x11, waiting for transfers between devices  53.1 us
    all_to_all x4, waiting for transfers between devices, exchange(): shaped = lax.all_to_all(shaped, 'yhi', 1, 1, tiled=True)  40.3 us
    reduce_scatter x2, waiting for transfers between devices, dp_reduce_scatter(): x = lax.psum_scatter(x, 'ylo', scatter_dimension=row_axis + 1, tiled=True)  39.8 us
    all_to_all x2, blocking collectives, exchange(): shaped = lax.all_to_all(shaped, 'x', 2, 2, tiled=True)  24.2 us
    all_to_all x4, starting transfers between devices, exchange(): shaped = lax.all_to_all(shaped, 'yhi', 1, 1, tiled=True)  23.7 us
  transfers between devices with their start and end apart: 16, of which 14 were waited for; matrix products, arithmetic and copies ran while one was open for 7% of the time, Pallas kernels for 0%

commit v1 on v0

--- a/solution.py
+++ b/solution.py
@@ -161,7 +161,8 @@
         0,
     ).transpose(1, 0, 2)
     rights = jnp.concatenate([right_up_term, right_down_term], axis=0)
-    rights = lax.psum(rights, DP_AXES)
+    pieces = lax.all_gather(rights, DP_AXES, axis=0, tiled=False)
+    rights = pieces.sum(axis=0)
     grad_up_right = rights[:group_up]
     grad_down_right = rights[group_up:]
     return (layer_out, grad_tokens, grad_up_left, grad_up_right, grad_down_left, grad_down_right)

time: 652 us -> 653 us (level)
  other arithmetic: 2.13 us -> 17.5 us
  waiting for transfers between devices: 509 us -> 498 us
    psum x1 -> x0, waiting for transfers between devices: 233 us -> none  [on_device(): rights = lax.psum(rights, DP_AXES)]
    all_gather x0 -> x1, waiting for transfers between devices: none -> 230 us  [on_device(): pieces = lax.all_gather(rights, DP_AXES, axis=0, tiled=False)]
    reduce_sum x0 -> x1, other arithmetic: none -> 14.9 us  [on_device(): rights = pieces.sum(axis=0)]
    reduce_scatter x2, waiting for transfers between devices: 39.8 us -> 29.4 us  [dp_reduce_scatter(): x = lax.psum_scatter(x, 'ylo', scatter_dimension=row_axis + 1, tiled=True)]
    all_to_all x4, waiting for transfers between devices: 40.3 us -> 47.1 us  [exchange(): shaped = lax.all_to_all(shaped, 'yhi', 1, 1, tiled=True)]
    unnamed x29 -> x31, local copies, waits for them, and re-layouts: 14.7 us -> 15.7 us
  transfers between devices with their start and end apart: 16 -> 16, of which waited for: 14 -> 14; matrix products, arithmetic and copies ran while one was open for 7% -> 8% of each run, Pallas kernels for 0% -> 0%
where the time goes in v1:
time: 653 us; the launch traced here: 652 us
  waiting for transfers between devices  498 us (76%)
  blocking collectives  35.8 us (5%)
  starting transfers between devices  31.5 us (5%)
  local copies, waits for them, and re-layouts  30.6 us (5%)
  matrix products  23.7 us (4%)
  other arithmetic  17.5 us (3%)
  between operations  14.4 us (2%)
    all_gather x1, waiting for transfers between devices, on_device(): pieces = lax.all_gather(rights, DP_AXES, axis=0, tiled=False)  230 us
    all_gather x2, waiting for transfers between devices, dp_all_gather(): x = lax.all_gather(x, 'z', axis=row_axis, tiled=True)  75 us
    reduce_scatter x2, waiting for transfers between devices, dp_reduce_scatter(): x = lax.psum_scatter(x, 'z', scatter_dimension=row_axis, tiled=True)  53.6 us
    unnamed x11, waiting for transfers between devices  48.5 us
    all_to_all x4, waiting for transfers between devices, exchange(): shaped = lax.all_to_all(shaped, 'yhi', 1, 1, tiled=True)  47.1 us
    reduce_scatter x2, waiting for transfers between devices, dp_reduce_scatter(): x = lax.psum_scatter(x, 'ylo', scatter_dimension=row_axis + 1, tiled=True)  29.4 us
    all_to_all x2, blocking collectives, exchange(): shaped = lax.all_to_all(shaped, 'x', 2, 2, tiled=True)  24.2 us
    all_to_all x4, starting transfers between devices, exchange(): shaped = lax.all_to_all(shaped, 'yhi', 1, 1, tiled=True)  23.7 us
  transfers between devices with their start and end apart: 16, of which 14 were waited for; matrix products, arithmetic and copies ran while one was open for 8% of the time, Pallas kernels for 0%

profile of v1, /device:TPU:1, one launch (start us, length us, event | category | flops | bytes accessed | tf_op | source)
XLA Modules:
  0.0 651.8 jit_solution(788091459115869922)
XLA Ops:
  7.2 6.3 all-gather
  13.6 42.4 %all-gather.15.cloned.1.call-done = bf16[16,16,2048]{2,1,0:T(8,128)(2,1)} async-done(((bf16[2,16,2048]{2,1,0:T(8,128)(2,1)}), bf16[16,16,2048]{2,1,0:T(8,128)(2,1)}) %all-gather.15.cloned.1.call-update) | async-done | bytes 1048592 | tf_op jit(solution)/shard_map/all_gather | solution.py:49
  56.1 5.3 all-gather.2
  61.4 0.9 copy.117
  62.4 1.4 fusion
  63.8 2.1 reshape.98
  65.8 0.3 convolution_convert_fusion.3
  66.2 0.7 copy.118
  66.9 4.0 all-to-all-start.4
  70.8 10.1 %all-gather.11.cloned.1.call-done = bf16[1,8,2,2,16,2048]{5,4,3,2,1,0:T(8,128)(2,1)} async-done(((bf16[1,8,2,1,16,2048]{5,4,3,2,1,0:T(8,128)(2,1)}), bf16[1,8,2,2,16,2048]{5,4,3,2,1,0:T(8,128)(2,1)}) %all-gather.11.cloned.1.call-update) | async-done | bytes 2097168 | tf_op jit(solution)/shard_map/all_gather | solution.py:50
  80.9 2.3 convolution_convert_fusion
  83.3 1.1 copy.109
  84.4 3.5 all-to-all-start
  87.9 32.6 %all-gather.17.cloned.1.call-done = bf16[16,64,512]{2,1,0:T(8,128)(2,1)} async-done(((bf16[2,64,512]{2,1,0:T(8,128)(2,1)}), bf16[16,64,512]{2,1,0:T(8,128)(2,1)}) %all-gather.17.cloned.1.call-update) | async-done | bytes 1048592 | tf_op jit(solution)/shard_map/all_gather | solution.py:49
  120.6 0.7 copy.119
  121.3 6.5 all-to-all-start.5
  127.8 1.0 copy.110
  128.8 6.9 %all-to-all-done.5 = bf16[256,4,4,32]{0,3,2,1:T(8,128)(2,1)S(1)} async-done(((bf16[256,4,4,32]{0,3,2,1:T(8,128)(2,1)}), bf16[256,4,4,32]{0,3,2,1:T(8,128)(2,1)S(1)}, u32[]{:S(2)}, u32[]{:S(2)}) %all-to-all-start.5) | async-done | bytes 262176 | tf_op jit(solution)/shard_map/all_to_all | solution.py:28
  135.7 4.2 all-to-all-start.1
  140.0 1.2 copy.122
  141.2 4.1 all-gather.13.cloned.1.call-done
  145.3 2.3 fusion.16
  147.6 18.1 %all-to-all-done.1 = bf16[256,4,4,128]{0,3,2,1:T(8,128)(2,1)} async-done(((bf16[256,4,4,128]{0,3,2,1:T(8,128)(2,1)}), bf16[256,4,4,128]{0,3,2,1:T(8,128)(2,1)}, u32[]{:S(2)}, u32[]{:S(2)}) %all-to-all-start.1) | async-done | bytes 1048608 | tf_op jit(solution)/shard_map/all_to_all | solution.py:28
  165.7 4.5 fusion.7
  170.2 1.0 copy-done.3
  171.2 0.4 fusion.8
  171.6 0.3 reshape.100
  171.9 0.3 copy.123
  172.3 15.0 %all_to_all.40 = bf16[256,4,4,128]{0,3,1,2:T(8,128)(2,1)S(1)} all-to-all(bf16[256,4,4,128]{0,3,1,2:T(8,128)(2,1)S(1)} %copy.123), channel_id=1, replica_groups=mesh['z'=8,'ylo'=2,'core'=2,'yhi'=4,'x'=4] {'x'}, dimensions={2} | all-to-all | bytes 2097152 | tf_op jit(solution)/shard_map/all_to_all | solution.py:27
  187.3 1.0 copy.124
  188.3 6.5 all-to-all-start.7
  194.8 0.3 copy.113
  195.2 1.0 copy-done.7
  196.1 2.7 multiply_bitcast_fusion
  198.9 5.4 copy.129
  204.3 15.9 %all-to-all-done.7 = bf16[256,4,4,128]{0,3,2,1:T(8,128)(2,1)S(1)} async-done(((bf16[256,4,4,128]{0,3,2,1:T(8,128)(2,1)}), bf16[256,4,4,128]{0,3,2,1:T(8,128)(2,1)S(1)}, u32[]{:S(2)}, u32[]{:S(2)}) %all-to-all-start.7) | async-done | bytes 1048608 | tf_op jit(solution)/shard_map/all_to_all | solution.py:28
  220.2 2.7 convolution_multiply_fusion
  222.9 0.0 reduce-scatter.13.cloned.1.call-start
  223.0 1.3 dynamic-slice
  224.2 48.3 %all-reduce.5.cloned.1.call-done = (f32[8,2,2,16,1,2048]{5,3,4,2,1,0:T(8,128)}, f32[8,2,2,64,1,512]{5,3,2,1,0,4:T(8,128)}) async-done(((f32[8,2,2,16,1,2048]{5,3,4,2,1,0:T(8,128)}, f32[8,2,2,64,1,512]{5,3,2,1,0,4:T(8,128)}), (f32[8,2,2,16,1,2048]{5,3,4,2,1,0:T(8,128)}, f32[8,2,2,64,1,512]{5,3,2,1,0,4:T(8,128)})) %all-reduce.5.cloned.1.call-update) | async-done | bytes 8388624
  272.6 3.8 constant_dynamic-slice_fusion
  276.5 3.8 constant_dynamic-slice_fusion.1
  280.3 1.6 copy-done.2
  281.9 1.9 fusion.9
  283.8 0.1 copy.114
  284.0 9.2 %all_to_all.41 = bf16[256,4,4,32]{0,3,1,2:T(8,128)(2,1)S(1)} all-to-all(bf16[256,4,4,32]{0,3,1,2:T(8,128)(2,1)S(1)} %copy.115), channel_id=1, replica_groups=mesh['z'=8,'ylo'=2,'core'=2,'yhi'=4,'x'=4] {'x'}, dimensions={2} | all-to-all | bytes 524288 | tf_op jit(solution)/shard_map/all_to_all | solution.py:27
  293.2 0.7 copy.116
  293.9 6.4 all-to-all-start.3
  300.4 0.1 copy.127
  300.5 2.0 convolution_multiply_fusion.1
  302.5 6.2 all-to-all-done.3
  308.7 0.4 convolution_multiply_fusion.2
  309.1 1.2 pad_maximum_fusion
  310.4 7.4 %reduce-scatter.13.cloned.1.call-done = f32[1,2,1,64,1,512]{5,3,2,1,0,4:T(8,128)} async-done(((f32[8,2,1,64,1,512]{5,3,2,1,0,4:T(8,128)}), f32[1,2,1,64,1,512]{5,3,2,1,0,4:T(8,128)}) %reduce-scatter.13.cloned.1.call-update) | async-done | bytes 262160 | tf_op jit(solution)/shard_map/reduce_scatter | solution.py:39
  317.8 46.2 %reduce-scatter.9.cloned.1.call-done = f32[1,2,1,16,1,2048]{5,3,4,2,1,0:T(8,128)} async-done(((f32[8,2,1,16,1,2048]{5,3,4,2,1,0:T(8,128)}), f32[1,2,1,16,1,2048]{5,3,4,2,1,0:T(8,128)}) %reduce-scatter.9.cloned.1.call-update) | async-done | bytes 262160 | tf_op jit(solution)/shard_map/reduce_scatter | solution.py:39
  364.1 1.0 convolution_convert_fusion.4
  365.2 3.0 convolution_convert_fusion.2
  368.2 230.4 %all-gather.19.cloned.1.call-done = f32[5120,16,16]{2,1,0:T(8,128)} async-done(((f32[160,16,16]{2,1,0:T(8,128)}), f32[5120,16,16]{2,1,0:T(8,128)}) %all-gather.19.cloned.1.call-update) | async-done | bytes 5242896 | tf_op jit(solution)/shard_map/all_gather | solution.py:164
  598.6 14.9 %reduce_sum.9 = f32[160,16,16]{2,1,0:T(8,128)S(1)} reduce(f32[32,160,16,16]{3,2,1,0:T(8,128)} %bitcast.116, f32[]{:T(128)} %constant.5.clone.1), dimensions={0}, to_apply=%region_3.0 | reduce | flops 1269760 | bytes 5406724 | tf_op jit(solution)/shard_map/reduce_sum | solution.py:165
  613.6 0.1 slice.8
  613.7 1.1 copy.130
  614.7 0.8 copy.131
  615.5 6.0 reduce-scatter.15.cloned.1.call-done
  621.5 23.4 %reduce-scatter.11.cloned.1.call-done = f32[1,1,1,16,1,2048]{5,3,4,2,1,0:T(8,128)} async-done(((f32[1,2,1,16,1,2048]{5,3,4,2,1,0:T(8,128)}), f32[1,1,1,16,1,2048]{5,3,4,2,1,0:T(8,128)}) %reduce-scatter.11.cloned.1.call-update) | async-done | bytes 131088 | tf_op jit(solution)/shard_map/reduce_scatter | solution.py:40
  (45 shorter events, 0.5 us)
Async XLA Ops:
  7.2 73.8 %copy-start = (bf16[256,512]{1,0:T(8,128)(2,1)S(1)}, bf16[256,512]{1,0:T(8,128)(2,1)}, u32[]{:S(2)}) copy-start(bf16[256,512]{1,0:T(8,128)(2,1)} %param.6) | copy-start | bytes 786436
  7.2 48.8 %all-gather.15.cloned.1.call-start = ((), (), s32[]{:S(2)}) async-start(), calls=%async_computation.18 | async-start | bytes 1179648 | tf_op jit(solution)/shard_map/all_gather | solution.py:49
  13.6 67.3 %all-gather.11.cloned.1.call-start = ((), (), s32[]{:S(2)}) async-start(), calls=%async_computation.12 | async-start | bytes 3145728 | tf_op jit(solution)/shard_map/all_gather | solution.py:50
  56.0 64.5 %all-gather.17.cloned.1.call-start = ((), (), s32[]{:S(2)}) async-start(), calls=%async_computation.19 | async-start | bytes 1179648 | tf_op jit(solution)/shard_map/all_gather | solution.py:49
  62.3 3.5 copy-start.10
  66.9 17.5 %all-to-all-start.4 = ((bf16[256,4,4,32]{0,3,1,2:T(8,128)(2,1)}), bf16[256,4,4,32]{0,3,1,2:T(8,128)(2,1)S(1)}, u32[]{:S(2)}, u32[]{:S(2)}) async-start(bf16[256,4,4,32]{0,3,1,2:T(8,128)(2,1)} %copy.118), calls=%async_computation.4 | async-start | bytes 524288 | tf_op jit(solution)/shard_map/all_to_all | solution.py:27
  84.4 37.0 %all-to-all-start = ((bf16[256,4,4,128]{0,3,1,2:T(8,128)(2,1)}), bf16[256,4,4,128]{0,3,1,2:T(8,128)(2,1)S(1)}, u32[]{:S(2)}, u32[]{:S(2)}) async-start(bf16[256,4,4,128]{0,3,1,2:T(8,128)(2,1)} %copy.109), calls=%async_computation | async-start | bytes 2097152 | tf_op jit(solution)/shard_map/all_to_all | solution.py:27
  87.9 57.4 %all-gather.13.cloned.1.call-start = ((), (), s32[]{:S(2)}) async-start(), calls=%async_computation.13 | async-start | bytes 3145728 | tf_op jit(solution)/shard_map/all_gather | solution.py:50
  121.3 14.4 %all-to-all-start.5 = ((bf16[256,4,4,32]{0,3,2,1:T(8,128)(2,1)}), bf16[256,4,4,32]{0,3,2,1:T(8,128)(2,1)S(1)}, u32[]{:S(2)}, u32[]{:S(2)}) async-start(bf16[256,4,4,32]{0,3,2,1:T(8,128)(2,1)} %copy.119), calls=%async_computation.5 | async-start | bytes 524288 | tf_op jit(solution)/shard_map/all_to_all | solution.py:28
  127.8 12.2 %copy-start.11 = (bf16[128,16,16]{0,2,1:T(8,128)(2,1)S(1)}, bf16[128,16,16]{0,2,1:T(8,128)(2,1)}, u32[]{:S(2)}) copy-start(bf16[128,16,16]{0,2,1:T(8,128)(2,1)} %param.8) | copy-start | bytes 196612
  135.7 30.0 %all-to-all-start.1 = ((bf16[256,4,4,128]{0,3,2,1:T(8,128)(2,1)}), bf16[256,4,4,128]{0,3,2,1:T(8,128)(2,1)}, u32[]{:S(2)}, u32[]{:S(2)}) async-start(bf16[256,4,4,128]{0,3,2,1:T(8,128)(2,1)} %copy.110), calls=%async_computation.1 | async-start | bytes 2097152 | tf_op jit(solution)/shard_map/all_to_all | solution.py:28
  165.7 5.5 copy-start.8
  170.2 1.0 copy-start.3
  187.3 7.5 %copy-start.9 = (bf16[256,16,128]{0,1,2:T(8,128)(2,1)S(1)}, bf16[256,16,128]{0,1,2:T(8,128)(2,1)}, u32[]{:S(2)}) copy-start(bf16[256,16,128]{0,1,2:T(8,128)(2,1)} %get-tuple-element.33) | copy-start | bytes 3145732
  188.3 31.9 %all-to-all-start.7 = ((bf16[256,4,4,128]{0,3,2,1:T(8,128)(2,1)}), bf16[256,4,4,128]{0,3,2,1:T(8,128)(2,1)S(1)}, u32[]{:S(2)}, u32[]{:S(2)}) async-start(bf16[256,4,4,128]{0,3,2,1:T(8,128)(2,1)} %copy.124), calls=%async_computation.7 | async-start | bytes 2097152 | tf_op jit(solution)/shard_map/all_to_all | solution.py:28
  194.8 77.7 %all-reduce.5.cloned.1.call-start = ((), (), s32[]{:S(2)}) async-start(), calls=%async_computation.21 | async-start | bytes 16777216
  195.2 1.0 copy-start.7
  220.2 2.7 copy-start.5
  222.9 94.8 %reduce-scatter.13.cloned.1.call-start = ((), (), s32[]{:S(2)}) async-start(), calls=%async_computation.16 | async-start | bytes 2359296 | tf_op jit(solution)/shard_map/reduce_scatter | solution.py:39
  276.4 87.7 %reduce-scatter.9.cloned.1.call-start = ((), (), s32[]{:S(2)}) async-start(), calls=%async_computation.14 | async-start | bytes 2359296 | tf_op jit(solution)/shard_map/reduce_scatter | solution.py:39
  280.3 1.6 copy-start.2
  283.8 16.7 %copy-start.4 = (bf16[256,16,128]{0,1,2:T(8,128)(2,1)S(1)}, bf16[256,16,128]{0,1,2:T(8,128)(2,1)}, u32[]{:S(2)}) copy-start(bf16[256,16,128]{0,1,2:T(8,128)(2,1)} %copy-done.3) | copy-start | bytes 3145732
  293.9 14.8 %all-to-all-start.3 = ((bf16[256,4,4,32]{0,3,2,1:T(8,128)(2,1)}), bf16[256,4,4,32]{0,3,2,1:T(8,128)(2,1)S(1)}, u32[]{:S(2)}, u32[]{:S(2)}) async-start(bf16[256,4,4,32]{0,3,2,1:T(8,128)(2,1)} %copy.116), calls=%async_computation.3 | async-start | bytes 524288 | tf_op jit(solution)/shard_map/all_to_all | solution.py:28
  300.4 298.2 %all-gather.19.cloned.1.call-start = ((), (), s32[]{:S(2)}) async-start(), calls=%async_computation.20 | async-start | bytes 43253760 | tf_op jit(solution)/shard_map/all_gather | solution.py:164
  310.3 54.9 %copy-start.6 = (bf16[256,4,4,128]{0,3,2,1:T(8,128)(2,1)S(1)}, bf16[256,4,4,128]{0,3,2,1:T(8,128)(2,1)}, u32[]{:S(2)}) copy-start(bf16[256,4,4,128]{0,3,2,1:T(8,128)(2,1)} %copy-done.5) | copy-start | bytes 3145732
  310.3 311.2 %reduce-scatter.15.cloned.1.call-start = ((), (), s32[]{:S(2)}) async-start(), calls=%async_computation.17 | async-start | bytes 393216 | tf_op jit(solution)/shard_map/reduce_scatter | solution.py:40
  317.8 327.1 %reduce-scatter.11.cloned.1.call-start = ((), (), s32[]{:S(2)}) async-start(), calls=%async_computation.15 | async-start | bytes 393216 | tf_op jit(solution)/shard_map/reduce_scatter | solution.py:40
  598.6 46.3 %copy-start.1 = (bf16[256,512]{1,0:T(8,128)(2,1)S(1)}, bf16[256,512]{1,0:T(8,128)(2,1)}, u32[]{:S(2)}) copy-start(bf16[256,512]{1,0:T(8,128)(2,1)} %param.6) | copy-start | bytes 786436
Sparse Core Ops, SparseCore 0:
  13.7 42.2 all-gather.14
  58.1 22.8 all-gather.10
  83.0 37.5 all-gather.16
  122.5 22.7 all-gather.12
  223.0 49.4 all-reduce.4
  276.5 41.1 reduce-scatter.12
  320.6 43.4 reduce-scatter.8
  366.2 232.3 all-gather.18
  601.9 19.5 reduce-scatter.14
  624.9 19.9 reduce-scatter.10
